TPU v7x, 512 devices: a whole 4x4x16 slice. The times are simulated.
512 devices in a mesh: attn: 64 (over y, z), dp: 4 (over x), tensor: 2 (over core).
Axes of the slice: x: 4, y: 4, z: 16, core: 2. Of those that a mesh axis runs over, the one named last changes fastest.
Arguments:
- hidden_state: bfloat16 [256, 8192], P('dp', 'attn'), may hold values from -6 to 6
- w_query: bfloat16 [8192, 8192], P('attn', 'tensor'), may hold values from -0.0625 to 0.0625
- w_keyval: bfloat16 [8192, 2, 1024], P('attn', None, 'tensor'), may hold values from -0.0625 to 0.0625
- w_output: bfloat16 [8192, 8192], P('tensor', 'attn'), may hold values from -0.0625 to 0.0625
- kv_cache: bfloat16 [4, 49152, 2, 8, 128], P('dp', 'attn', None, 'tensor'), as said below
- lengths: int32 [4, 64], P('dp'), may hold values from 1 to 256, 8192 in all within a row
- owner_of: int32 [4, 64, 1], P('dp'), may hold values from 0 to 63; in each aligned block of 64 rows (0 to 63, 64 to 127, ..., all dimensions but the last counted through in order) at most 3 rows name the same one
Outputs:
- attended: bfloat16 [256, 8192], P('dp', 'attn')
Inputs may be any that keep to these rules, and one draw needn't show every extreme that they name: `owner_of`: in each data group at most 3 requests are placed on one attention device, and in some groups exactly 3 on one. The lengths of each data group sum to 8192, and the longest is exactly 256. `kv_cache`: finite keys and values.
All inputs are finite; a program needn't handle non-finite values.
Results may differ from a plain program's by a relative error of at most 0.009.
The roundings to bfloat16 on the way count: a program that leaves them out, or rounds other values in their place, can miss the bound.
Values may be sent and summed in bfloat16 or wider, within the bound.
No kernel may reach another device: no remote copies, remote signals or barrier semaphores. Data moves between devices by JAX's collectives and lax.ppermute only.
A program may use at most 64 MiB of HBM per device.

v0:
```python
import math
import jax
import jax.numpy as jnp
from jax import lax
from jax.sharding import PartitionSpec as P

HD = 128
CAP = 3
ROPE_BASE = 500000.0


def rotate_pairs(vectors, positions):
    half_dim = vectors.shape[-1] // 2
    steps_f = jnp.arange(half_dim).astype(jnp.float32) * (2.0 / vectors.shape[-1])
    inv_freq = jnp.exp(-math.log(ROPE_BASE) * steps_f)
    angles = positions[:, None] * inv_freq[None, :]
    cosine = jnp.cos(angles)[:, None, :]
    sine_part = jnp.sin(angles)[:, None, :]
    front_half = vectors[..., :half_dim]
    back_half = vectors[..., half_dim:]
    return jnp.concatenate(
        [front_half * cosine - back_half * sine_part, back_half * cosine + front_half * sine_part],
        axis=-1,
    )


def finish(query_part, keyval_part, positions, heads_loc, kv_loc):
    row_count = query_part.shape[0]
    query_rot = rotate_pairs(query_part.reshape(row_count, heads_loc, HD), positions).astype(
        jnp.bfloat16
    )
    keyval = keyval_part.reshape(row_count, 2, kv_loc, HD)
    key_rot = rotate_pairs(keyval[:, 0], positions).astype(jnp.bfloat16)
    val_new = keyval[:, 1].astype(jnp.bfloat16)
    packed = jnp.stack([key_rot, val_new], axis=1).reshape(row_count, 2 * kv_loc * HD)
    return (query_rot.reshape(row_count, heads_loc * HD), packed)


def local(hidden_state, w_query, w_keyval, w_output, kv_cache, lengths, owner_of):
    rows_group = hidden_state.shape[0]
    width_loc = hidden_state.shape[1]
    my_index = lax.axis_index("attn")
    heads_loc = w_query.shape[1] // HD
    kv_loc = w_keyval.shape[2] // HD
    group_size = heads_loc // kv_loc
    score_scale = 1.0 / math.sqrt(HD)
    query_part = jnp.dot(hidden_state, w_query, preferred_element_type=jnp.float32)
    keyval_part = jnp.dot(
        hidden_state,
        w_keyval.reshape(width_loc, 2 * kv_loc * HD),
        preferred_element_type=jnp.float32,
    )
    owners = owner_of.reshape(rows_group)
    req_lens = lengths.reshape(rows_group)
    req_order = jnp.arange(rows_group, dtype=jnp.int32)
    same_owner = owners[:, None] == owners[None, :]
    earlier = req_order[None, :] < req_order[:, None]
    before_mine = same_owner & earlier
    starts = jnp.sum(jnp.where(before_mine, req_lens[None, :], 0), axis=1)
    slot_rank = jnp.sum(before_mine.astype(jnp.int32), axis=1)
    positions = req_lens.astype(jnp.float32)
    query_sum, keyval_sum = lax.psum((query_part, keyval_part), "attn")
    query_rows, keyval_rows = finish(query_sum, keyval_sum, positions, heads_loc, kv_loc)
    slot_hit = (owners[None, :] == my_index) & (
        slot_rank[None, :] == jnp.arange(CAP, dtype=jnp.int32)[:, None]
    )
    chosen = jnp.sum(jnp.where(slot_hit, req_order[None, :], 0), axis=1)
    present = jnp.any(slot_hit, axis=1)
    my_start = jnp.take(starts, chosen)
    my_len = jnp.where(present, jnp.take(req_lens, chosen), 0)
    query_mine = jnp.take(query_rows, chosen, axis=0)
    keyval_mine = jnp.take(keyval_rows, chosen, axis=0).reshape(CAP, 2, kv_loc, HD)
    cache_local = kv_cache[0]
    grouped = query_mine.reshape(CAP, kv_loc, group_size, HD)
    scores = (
        jnp.einsum("ckgd,skd->ckgs", grouped, cache_local[:, 0], preferred_element_type=jnp.float32)
        * score_scale
    )
    own_score = (
        jnp.einsum("ckgd,ckd->ckg", grouped, keyval_mine[:, 0], preferred_element_type=jnp.float32)
        * score_scale
    )
    slot_pos = jnp.arange(cache_local.shape[0], dtype=jnp.int32)
    live = (slot_pos[None, :] >= my_start[:, None]) & (
        slot_pos[None, :] < (my_start + my_len)[:, None]
    )
    live = live[:, None, None, :]
    row_max = jnp.maximum(jnp.max(jnp.where(live, scores, -jnp.inf), axis=-1), own_score)
    weights = jnp.where(live, jnp.exp(scores - row_max[..., None]), 0.0)
    own_weight = jnp.exp(own_score - row_max)
    total_weight = jnp.sum(weights, axis=-1) + own_weight
    probs = (weights / total_weight[..., None]).astype(jnp.bfloat16)
    own_prob = (own_weight / total_weight).astype(jnp.bfloat16)
    mixed = jnp.einsum(
        "ckgs,skd->ckgd", probs, cache_local[:, 1], preferred_element_type=jnp.float32
    )
    mixed = (
        mixed
        + own_prob.astype(jnp.float32)[..., None]
        * keyval_mine[:, 1].astype(jnp.float32)[:, :, None, :]
    )
    out_slots = mixed.reshape(CAP, heads_loc * HD).astype(jnp.bfloat16)
    gathered = lax.all_gather(out_slots, "attn", axis=0, tiled=True)
    heads_out = jnp.take(gathered, owners * CAP + slot_rank, axis=0)
    out_part = jnp.dot(heads_out, w_output, preferred_element_type=jnp.float32)
    out_total = lax.psum(out_part, "tensor")
    return out_total.astype(jnp.bfloat16)


def solution(mesh):
    placed = (
        P("dp", "attn"),
        P("attn", "tensor"),
        P("attn", None, "tensor"),
        P("tensor", "attn"),
        P("dp", "attn", None, "tensor", None),
        P("dp", None),
        P("dp", None, None),
    )
    return jax.shard_map(
        local, mesh=mesh, in_specs=placed, out_specs=P("dp", "attn"), check_vma=False
    )
```

profile of v0, /device:TPU:1, one launch (start us, length us, event | category | flops | bytes accessed | tf_op | source)
XLA Modules:
  0.0 454.5 jit_solution(9612542293275163695)
XLA Ops:
  6.5 0.0 copy-start
  6.5 0.0 all-reduce.3.cloned.1.call-start
  6.5 1.2 copy-done
  7.8 1.0 convolution_bitcast_fusion
  8.8 0.0 copy-start.5
  8.8 0.0 copy-start.6
  8.8 1.2 copy.37
  10.0 0.0 copy-start.1
  10.0 0.0 copy-start.7
  10.0 0.0 copy-done.5
  10.0 0.0 copy-done.6
  10.0 0.2 fusion.30
  10.2 0.0 copy-start.4
  10.2 0.8 reshape.238
  11.0 0.0 all-reduce.3.cloned.1.call-update
  11.1 0.0 all-gather.3.cloned.1.call-start
  11.1 0.0 copy-done.1
  11.1 0.0 copy-done.7
  11.1 0.2 select_reduce_fusion.1
  11.3 0.1 select_reduce_fusion.2
  11.5 0.6 gather_fusion.4
  12.1 0.6 gather_fusion.3
  12.8 0.0 copy-done.4
  12.8 1.4 copy.65
  14.1 0.1 fusion.24
  14.3 0.1 fusion.17
  14.4 0.2 multiply_cosine_fusion
  14.6 269.9 %all-reduce.3.cloned.1.call-done = (f32[64,32,128]{2,1,0:T(8,128)}, f32[64,2,4,128]{3,2,1,0:T(4,128)}) async-done(((f32[64,32,128]{2,1,0:T(8,128)}, f32[64,2,4,128]{3,2,1,0:T(4,128)}), (f32[64,32,128]{2,1,0:T(8,128)}, f32[64,2,4,128]{3,2,1,0:T(4,128)})) %all-reduce.3.cloned.1.call-update) | async-done | bytes 1310736 | tf_op jit(solution)/shard_map/psum | solution.py:62
  284.5 0.0 copy-start.2
  284.5 1.0 slice_bitcast_fusion.4
  285.5 0.9 slice.87
  286.4 0.2 fusion.12
  286.6 0.1 pad_maximum_fusion.1
  286.7 0.1 reshape.239
  286.8 0.6 gather_fusion.1
  287.4 0.1 broadcast_select_fusion
  287.5 0.0 copy-done.2
  287.5 0.5 subtract_convert_fusion
  287.9 0.0 copy-start.3
  288.0 0.3 pad_maximum_fusion
  288.3 0.2 copy.66
  288.5 0.6 gather_fusion
  289.1 0.1 copy_select_fusion
  289.1 0.1 fusion.15
  289.3 0.1 copy-done.3
  289.4 0.4 select_reduce_fusion
  289.8 0.2 fusion.7
  290.0 0.3 fusion.2
  290.3 0.6 reshape.283
  290.9 0.0 all-gather.3.cloned.1.call-update
  291.0 136.5 %all-gather.3.cloned.1.call-done = bf16[64,3,4096]{2,1,0:T(4,128)(2,1)} async-done(((bf16[1,3,4096]{2,1,0:T(4,128)(2,1)}), bf16[64,3,4096]{2,1,0:T(4,128)(2,1)}) %all-gather.3.cloned.1.call-update) | async-done | bytes 1572880 | tf_op jit(solution)/shard_map/all_gather | solution.py:103
  427.5 3.1 reshape.284
  430.6 0.9 gather_fusion.2
  431.5 1.6 fusion.3
  433.1 14.6 %psum.23 = bf16[64,128]{1,0:T(8,128)(2,1)} all-reduce(f32[64,128]{1,0:T(8,128)S(1)} %fusion.3), channel_id=1, replica_groups=mesh['attn'=64,'dp'=4,'tensor'=2] {'tensor'}, use_global_device_ids=true, to_apply=%region_8.10 | all-reduce | flops 8192 | bytes 49152 | tf_op jit(solution)/shard_map/psum | solution.py:106
  (16 shorter events, 0.1 us)
Async XLA Ops:
  6.5 1.2 copy-start
  6.5 277.9 %all-reduce.3.cloned.1.call-start = ((), (), s32[]{:S(2)}) async-start(), calls=%async_computation.1 | async-start | bytes 2621440 | tf_op jit(solution)/shard_map/psum | solution.py:62
  8.8 1.2 copy-start.5
  8.8 1.2 copy-start.6
  10.0 1.1 copy-start.1
  10.0 1.2 copy-start.7
  10.2 2.6 copy-start.4
  11.1 416.4 %all-gather.3.cloned.1.call-start = ((), (), s32[]{:S(2)}) async-start(), calls=%async_computation | async-start | bytes 2129920 | tf_op jit(solution)/shard_map/all_gather | solution.py:103
  284.5 3.0 copy-start.2
  287.9 1.4 copy-start.3
Sparse Core Ops, SparseCore 0:
  11.2 273.2 all-reduce.2
  291.1 136.3 all-gather.2
where the time goes:
time: 455 us
  waiting for transfers between devices  406 us (89%)
  blocking collectives  14.6 us (3%)
  local copies, waits for them, and re-layouts  14 us (3%)
  between operations  13.7 us (3%)
    psum x1, waiting for transfers between devices, local(): query_sum, keyval_sum = lax.psum((query_part, keyval_part), 'attn')  270 us
    all_gather x1, waiting for transfers between devices, local(): gathered = lax.all_gather(out_slots, 'attn', axis=0, tiled=True)  137 us
    psum x1, blocking collectives, local(): out_total = lax.psum(out_part, 'tensor')  14.6 us
  transfers between devices with their start and end apart: 2, of which 2 were waited for; matrix products, arithmetic and copies ran while one was open for 1% of the time, Pallas kernels for 0%

commit v1 on v0

--- a/solution.py
+++ b/solution.py
@@ -100,7 +100,9 @@
         * keyval_mine[:, 1].astype(jnp.float32)[:, :, None, :]
     )
     out_slots = mixed.reshape(CAP, heads_loc * HD).astype(jnp.bfloat16)
-    gathered = lax.all_gather(out_slots, "attn", axis=0, tiled=True)
+    gathered = jnp.concatenate(
+        lax.all_to_all(jnp.stack([out_slots] * lax.axis_size("attn")), "attn", 0, 0), axis=0
+    )
     heads_out = jnp.take(gathered, owners * CAP + slot_rank, axis=0)
     out_part = jnp.dot(heads_out, w_output, preferred_element_type=jnp.float32)
     out_total = lax.psum(out_part, "tensor")

time: 455 us -> 416 us (0.914)
  waiting for transfers between devices: 406 us -> 352 us
  starting transfers between devices: 0.04 us -> 9.05 us
    all_gather x1 -> x0, waiting for transfers between devices: 137 us -> none  [local(): gathered = lax.all_gather(out_slots, 'attn', axis=0, tiled=True)]
    all_to_all x0 -> x1, waiting for transfers between devices: none -> 82.3 us  [local(): lax.all_to_all(jnp.stack([out_slots] * lax.axis_size('attn')), 'attn', 0, 0)]
    all_to_all x0 -> x1, starting transfers between devices: none -> 9.05 us  [local(): lax.all_to_all(jnp.stack([out_slots] * lax.axis_size('attn')), 'attn', 0, 0)]
where the time goes in v1:
time: 416 us
  waiting for transfers between devices  352 us (85%)
  blocking collectives  19.1 us (5%)
  local copies, waits for them, and re-layouts  15.7 us (4%)
  between operations  13.7 us (3%)
  starting transfers between devices  9.05 us (2%)
    psum x1, waiting for transfers between devices, local(): query_sum, keyval_sum = lax.psum((query_part, keyval_part), 'attn')  270 us
    all_to_all x1, waiting for transfers between devices, local(): lax.all_to_all(jnp.stack([out_slots] * lax.axis_size('attn')), 'attn', 0, 0)  82.3 us
    psum x1, blocking collectives, local(): out_total = lax.psum(out_part, 'tensor')  19.1 us
    all_to_all x1, starting transfers between devices, local(): lax.all_to_all(jnp.stack([out_slots] * lax.axis_size('attn')), 'attn', 0, 0)  9.05 us
  transfers between devices with their start and end apart: 2, of which 2 were waited for; matrix products, arithmetic and copies ran while one was open for 1% of the time, Pallas kernels for 0%

profile of v1, /device:TPU:1, one launch (start us, length us, event | category | flops | bytes accessed | tf_op | source)
XLA Modules:
  0.0 415.6 jit_solution(16606112919233886089)
XLA Ops:
  6.5 0.0 copy-start
  6.5 0.0 all-reduce.3.cloned.1.call-start
  6.5 1.2 copy-done
  7.8 1.0 convolution_bitcast_fusion
  8.8 0.0 copy-start.5
  8.8 0.0 copy-start.6
  8.8 1.2 copy.31
  10.0 0.0 copy-start.1
  10.0 0.0 copy-start.7
  10.0 0.0 copy-done.5
  10.0 0.0 copy-done.6
  10.0 0.2 fusion.30
  10.2 0.0 copy-start.4
  10.2 0.8 reshape.244
  11.0 0.0 all-reduce.3.cloned.1.call-update
  11.1 0.0 copy-done.1
  11.1 0.0 copy-done.7
  11.1 0.2 select_reduce_fusion.1
  11.3 0.1 select_reduce_fusion.2
  11.4 0.6 gather_fusion.4
  12.1 0.6 gather_fusion.3
  12.7 0.0 copy-done.4
  12.7 1.4 copy.62
  14.1 0.1 fusion.24
  14.3 0.1 fusion.17
  14.3 0.2 multiply_cosine_fusion
  14.5 269.9 %all-reduce.3.cloned.1.call-done = (f32[64,32,128]{2,1,0:T(8,128)}, f32[64,2,4,128]{3,2,1,0:T(4,128)}) async-done(((f32[64,32,128]{2,1,0:T(8,128)}, f32[64,2,4,128]{3,2,1,0:T(4,128)}), (f32[64,32,128]{2,1,0:T(8,128)}, f32[64,2,4,128]{3,2,1,0:T(4,128)})) %all-reduce.3.cloned.1.call-update) | async-done | bytes 1310736 | tf_op jit(solution)/shard_map/psum | solution.py:62
  284.4 0.0 copy-start.2
  284.4 1.0 slice_bitcast_fusion.4
  285.4 0.9 slice.87
  286.4 0.2 fusion.12
  286.5 0.1 pad_maximum_fusion.1
  286.7 0.1 reshape.245
  286.8 0.6 gather_fusion.1
  287.3 0.1 broadcast_select_fusion
  287.4 0.0 copy-done.2
  287.4 0.5 subtract_convert_fusion
  287.9 0.0 copy-start.3
  287.9 0.3 pad_maximum_fusion
  288.2 0.2 copy.63
  288.4 0.6 gather_fusion
  289.0 0.1 copy_select_fusion
  289.1 0.1 fusion.15
  289.2 0.1 copy-done.3
  289.3 0.4 select_reduce_fusion
  289.7 0.2 fusion.7
  290.0 0.3 fusion.2
  290.3 2.3 stack.5
  292.6 9.1 %all-to-all-start = ((bf16[64,3,4096]{2,1,0:T(4,128)(2,1)}), bf16[64,3,4096]{2,1,0:T(4,128)(2,1)}, u32[]{:S(2)}, u32[]{:S(2)}) async-start(bf16[64,3,4096]{2,1,0:T(4,128)(2,1)} %stack.5), calls=%async_computation | async-start | bytes 4194304 | tf_op jit(solution)/shard_map/all_to_all | solution.py:104
  301.7 82.3 %all-to-all-done = bf16[64,3,4096]{2,1,0:T(4,128)(2,1)} async-done(((bf16[64,3,4096]{2,1,0:T(4,128)(2,1)}), bf16[64,3,4096]{2,1,0:T(4,128)(2,1)}, u32[]{:S(2)}, u32[]{:S(2)}) %all-to-all-start) | async-done | bytes 1572896 | tf_op jit(solution)/shard_map/all_to_all | solution.py:104
  384.0 3.1 reshape.246
  387.2 0.9 gather_fusion.2
  388.1 1.6 fusion.3
  389.7 19.1 %psum.23 = bf16[64,128]{1,0:T(8,128)(2,1)} all-reduce(f32[64,128]{1,0:T(8,128)S(1)} %fusion.3), channel_id=1, replica_groups=mesh['attn'=64,'dp'=4,'tensor'=2] {'tensor'}, use_global_device_ids=true, to_apply=%region_8.10 | all-reduce | flops 8192 | bytes 49152 | tf_op jit(solution)/shard_map/psum | solution.py:108
  (17 shorter events, 0.2 us)
Async XLA Ops:
  6.5 1.2 copy-start
  6.5 277.9 %all-reduce.3.cloned.1.call-start = ((), (), s32[]{:S(2)}) async-start(), calls=%async_computation.1 | async-start | bytes 2621440 | tf_op jit(solution)/shard_map/psum | solution.py:62
  8.8 1.2 copy-start.5
  8.8 1.2 copy-start.6
  10.0 1.1 copy-start.1
  10.0 1.1 copy-start.7
  10.2 2.5 copy-start.4
  284.4 3.0 copy-start.2
  287.9 1.4 copy-start.3
  292.6 91.4 %all-to-all-start = ((bf16[64,3,4096]{2,1,0:T(4,128)(2,1)}), bf16[64,3,4096]{2,1,0:T(4,128)(2,1)}, u32[]{:S(2)}, u32[]{:S(2)}) async-start(bf16[64,3,4096]{2,1,0:T(4,128)(2,1)} %stack.5), calls=%async_computation | async-start | bytes 4194304 | tf_op jit(solution)/shard_map/all_to_all | solution.py:104
Sparse Core Ops, SparseCore 0:
  11.2 273.1 all-reduce.2
